TPU v7x, 512 devices: a whole 4x4x16 slice. The times are simulated.
512 devices in a mesh: dp: 64 (over z, x), pair: 8 (over y, core).
Axes of the slice: x: 4, y: 4, z: 16, core: 2. Of those that a mesh axis runs over, the one named last changes fastest.
Arguments:
- embedding: bfloat16 [65536, 1024], P(('dp', 'pair')), may hold values from -32 to 32
- labels: int32 [65536], P(('dp', 'pair')), may hold values from 0 to 127, as said below
- order_ids: int32 [65536], P(('dp', 'pair')), may hold values from 0 to 65535, each once
Outputs:
- best_similarity: float32 [65536], P(('dp', 'pair'))
Inputs may be any that keep to these rules, and one draw needn't show every extreme that they name: `labels`: clusters 2 * g to 2 * g + 1 form owner group g. Among the 128 rows of one device (aligned blocks of the whole array) at most 4 name clusters of any one group, and in every draw some group gets exactly 4 rows from every device.
All inputs are finite; a program needn't handle non-finite values.
Results may differ from a plain program's by a relative error of at most 0.00049.
Values may be sent and summed in bfloat16 or wider, within the bound.
No kernel may reach another device: no remote copies, remote signals or barrier semaphores. Data moves between devices by JAX's collectives and lax.ppermute only.
A program may use at most 64 MiB of HBM per device.

v0:
```python
import jax
import jax.numpy as jnp
from jax import lax
from jax.sharding import PartitionSpec as P

CL_OWN = 2


def tile_best(own_rows, own_labels, own_order, other_rows, other_labels, other_order):
    scores = jnp.dot(own_rows, other_rows.T, preferred_element_type=jnp.float32)
    same_cluster = (other_labels[None, :] == own_labels[:, None]) & (own_labels[:, None] >= 0)
    earlier = same_cluster & (other_order[None, :] < own_order[:, None])
    after_own = same_cluster & (own_order[:, None] < other_order[None, :])
    ahead = jnp.max(jnp.where(earlier, scores, -1.0), axis=1)
    behind = jnp.max(jnp.where(after_own, scores, -1.0), axis=0)
    return (ahead, behind)


def on_device(embedding, labels, order_ids):
    groups = lax.axis_size("dp")
    rows_here = embedding.shape[0]
    capacity = 2 * rows_here // groups
    slot_count = groups * capacity
    values = embedding.astype(jnp.float32)
    squares = jnp.sum(values * values, axis=1, keepdims=True)
    shifted = squares + 1e-06
    unit_rows = (values * lax.rsqrt(shifted)).astype(jnp.bfloat16)
    owner_group = labels // CL_OWN
    onehot = (owner_group[:, None] == jnp.arange(groups, dtype=jnp.int32)[None, :]).astype(
        jnp.int32
    )
    before = jnp.cumsum(onehot, axis=0) - onehot
    slot_index = owner_group * capacity + jnp.sum(before * onehot, axis=1)
    send_rows = (
        jnp.zeros((slot_count, unit_rows.shape[1]), jnp.bfloat16).at[slot_index].set(unit_rows)
    )
    send_labels = jnp.full((slot_count,), -1, jnp.int32).at[slot_index].set(labels)
    send_order = jnp.zeros((slot_count,), jnp.int32).at[slot_index].set(order_ids)
    got_rows, got_labels, got_order = (
        lax.all_to_all(
            send_rows.reshape(groups, capacity, -1), "dp", split_axis=0, concat_axis=0, tiled=True
        ),
        lax.all_to_all(
            send_labels.reshape(groups, capacity), "dp", split_axis=0, concat_axis=0, tiled=True
        ),
        lax.all_to_all(
            send_order.reshape(groups, capacity), "dp", split_axis=0, concat_axis=0, tiled=True
        ),
    )
    got_rows = got_rows.reshape(slot_count, -1)
    got_labels = got_labels.reshape(slot_count)
    got_order = got_order.reshape(slot_count)
    best_seen = jnp.full((slot_count,), -1.0, jnp.float32)
    piece = (
        lax.all_gather(got_rows, "pair", axis=0, tiled=True),
        lax.all_gather(got_labels, "pair", axis=0, tiled=True),
        lax.all_gather(got_order, "pair", axis=0, tiled=True),
    )
    piece_count = piece[0].shape[0]
    for offset in range(0, piece_count, 512):
        width_now = min(512, piece_count - offset)
        found = tile_best(
            got_rows,
            got_labels,
            got_order,
            piece[0][offset : offset + width_now],
            piece[1][offset : offset + width_now],
            piece[2][offset : offset + width_now],
        )
        best_seen = jnp.maximum(best_seen, found[0])
    answered = lax.all_to_all(
        best_seen.reshape(groups, capacity), "dp", split_axis=0, concat_axis=0, tiled=True
    )
    return answered.reshape(slot_count)[slot_index]


def solution(mesh):
    in_specs = (P(("dp", "pair"), None), P(("dp", "pair")), P(("dp", "pair")))
    out_specs = P(("dp", "pair"))
    return jax.shard_map(
        on_device, mesh=mesh, in_specs=in_specs, out_specs=out_specs, check_vma=False
    )
```

profile of v0, /device:TPU:8, one launch (start us, length us, event | category | flops | bytes accessed | tf_op | source)
XLA Modules:
  0.0 161.8 jit_solution(7379392571141710078)
XLA Ops:
  6.5 0.0 all-gather.4.cloned.1.call-start
  6.5 0.7 and_select_fusion
  7.2 1.1 fusion.8
  8.3 0.1 fusion.14
  8.4 0.2 reduce_window_sum.11
  8.6 0.2 select_reduce_fusion
  8.7 0.7 compare_select_fusion
  9.4 1.8 %scatter_custom_fusion.2 = bf16[256,1024]{1,0:T(8,128)(2,1)S(1)} fusion(s32[128]{0:T(128)S(1)} %compare_select_fusion, bf16[128,1024]{1,0:T(8,128)(2,1)} %param.3, f32[128]{0:T(128)S(1)} %add_rsqrt_fusion, bf16[]{:T(256)} %constant.18.clone.1), kind=kCustom, calls=%fused_computation.20 | custom fusion | flops 393216 | bytes 786946 | tf_op jit(solution)/shard_map/scatter | solution.py:35
  11.2 0.2 reshape.107
  11.4 51.2 %all_to_all.29 = bf16[64,4,1024]{2,1,0:T(4,128)(2,1)S(1)} all-to-all(bf16[64,4,1024]{2,1,0:T(4,128)(2,1)S(1)} %reshape.107), channel_id=1, replica_groups=mesh['dp'=64,'pair'=8] {'dp'}, dimensions={0} | all-to-all | bytes 1048576 | tf_op jit(solution)/shard_map/all_to_all | solution.py:40
  62.6 0.9 reshape.108
  63.5 0.0 copy-start
  63.5 0.0 all-gather.4.cloned.1.call-update
  63.5 1.2 scatter_custom_fusion
  64.8 0.7 all_to_all.19
  65.5 5.8 %all-to-all-start = ((s32[64,1,4]{2,1,0:T(1,128)}), s32[64,1,4]{2,1,0:T(1,128)S(1)}, u32[]{:S(2)}, u32[]{:S(2)}) async-start(s32[64,1,4]{2,1,0:T(1,128)} %bitcast), calls=%async_computation | async-start | bytes 65536 | tf_op jit(solution)/shard_map/all_to_all | solution.py:43
  71.3 1.1 scatter_custom_fusion.1
  72.4 0.7 all_to_all.21
  73.2 12.9 %all-to-all-done = s32[64,1,4]{2,1,0:T(1,128)S(1)} async-done(((s32[64,1,4]{2,1,0:T(1,128)}), s32[64,1,4]{2,1,0:T(1,128)S(1)}, u32[]{:S(2)}, u32[]{:S(2)}) %all-to-all-start) | async-done | bytes 1056 | tf_op jit(solution)/shard_map/all_to_all | solution.py:43
  86.1 4.5 %all-to-all-start.1 = ((s32[64,1,4]{2,1,0:T(1,128)}), s32[64,1,4]{2,1,0:T(1,128)S(1)}, u32[]{:S(2)}, u32[]{:S(2)}) async-start(s32[64,1,4]{2,1,0:T(1,128)} %bitcast.2), calls=%async_computation.1 | async-start | bytes 65536 | tf_op jit(solution)/shard_map/all_to_all | solution.py:46
  90.6 0.1 reshape.105
  90.7 14.5 %all-to-all-done.1 = s32[64,1,4]{2,1,0:T(1,128)S(1)} async-done(((s32[64,1,4]{2,1,0:T(1,128)}), s32[64,1,4]{2,1,0:T(1,128)S(1)}, u32[]{:S(2)}, u32[]{:S(2)}) %all-to-all-start.1) | async-done | bytes 1056 | tf_op jit(solution)/shard_map/all_to_all | solution.py:46
  105.2 0.1 reshape.106
  105.3 0.5 broadcast.74
  105.8 0.7 reduce.13
  106.6 0.1 reshape.148
  106.7 0.7 reduce.14
  107.4 0.1 reshape.146
  107.5 8.8 %all-gather = s32[8,1,256]{2,1,0:T(1,128)S(1)} all-gather(s32[1,1,256]{2,1,0:T(1,128)S(1)} %reshape.146), channel_id=1, replica_groups=mesh['dp'=64,'pair'=8] {'pair'}, dimensions={0}, use_global_device_ids=true | all-gather | bytes 9216 | tf_op jit(solution)/shard_map/all_gather | solution.py:56
  116.3 10.3 %all-gather.1 = s32[8,1,256]{2,1,0:T(1,128)S(1)} all-gather(s32[1,1,256]{2,1,0:T(1,128)S(1)} %reshape.148), channel_id=1, replica_groups=mesh['dp'=64,'pair'=8] {'pair'}, dimensions={0}, use_global_device_ids=true | all-gather | bytes 9216 | tf_op jit(solution)/shard_map/all_gather | solution.py:57
  126.6 0.0 all-gather.4.cloned.1.call-done
  126.6 0.0 copy-start.1
  126.6 2.1 %fusion.3 = f32[256]{0:T(256)S(1)} fusion(bf16[256,1024]{1,0:T(8,128)(2,1)} %reshape.108, bf16[2048,1024]{1,0:T(8,128)(2,1)} %all-gather.4.cloned.1.call-done, s32[512]{0:T(512)S(1)} %bitcast.29, s32[512]{0:T(512)S(1)} %bitcast.26, pred[256]{0:T(512)(128)(4,1)S(1)} %broadcast_compare_fusion, s32[256]{0:T(256)S(1)} %reshape.106, s32[256]{0:T(256)S(1)} %reshape.105), kind=kOutput, calls=%fused_computation.11 | convolution fusion | flops 269221632 | bytes 1580288 | tf_op jit(solution)/shard_map/dot_general | solution.py:10
  128.7 0.0 copy-done
  128.7 1.8 %fusion.2 = f32[256]{0:T(256)S(1)} fusion(bf16[256,1024]{1,0:T(8,128)(2,1)S(1)} %copy-done, bf16[2048,1024]{1,0:T(8,128)(2,1)} %all-gather.4.cloned.1.call-done, s32[512]{0:T(512)S(1)} %bitcast.28, s32[512]{0:T(512)S(1)} %bitcast.25, pred[256]{0:T(512)(128)(4,1)S(1)} %broadcast_compare_fusion, s32[256]{0:T(256)S(1)} %reshape.106, s32[256]{0:T(256)S(1)} %reshape.105), kind=kOutput, calls=%fused_computation.10 | convolution fusion | flops 269221632 | bytes 1580288 | tf_op jit(solution)/shard_map/dot_general | solution.py:10
  130.5 0.0 copy-done.1
  130.5 0.6 fusion.1
  131.1 0.6 fusion
  131.7 0.7 max.41
  132.4 4.6 %all-to-all-start.3 = ((f32[64,1,4]{2,1,0:T(1,128)}), f32[64,1,4]{2,1,0:T(1,128)S(1)}, u32[]{:S(2)}, u32[]{:S(2)}) async-start(f32[64,1,4]{2,1,0:T(1,128)} %bitcast.10), calls=%async_computation.3 | async-start | bytes 65536 | tf_op jit(solution)/shard_map/all_to_all | solution.py:71
  137.1 14.8 %all-to-all-done.3 = f32[64,1,4]{2,1,0:T(1,128)S(1)} async-done(((f32[64,1,4]{2,1,0:T(1,128)}), f32[64,1,4]{2,1,0:T(1,128)S(1)}, u32[]{:S(2)}, u32[]{:S(2)}) %all-to-all-start.3) | async-done | bytes 1056 | tf_op jit(solution)/shard_map/all_to_all | solution.py:71
  151.8 0.5 broadcast.76
  152.3 0.7 reduce.15
  153.1 0.1 reshape.109
  153.2 1.8 %gather_fusion = f32[128]{0:T(128)} fusion(f32[256]{0:T(256)S(1)} %reshape.109, s32[1024]{0:T(1024)S(1)} %pad_clamp_fusion), kind=kCustom, calls=%fused_computation | custom fusion | bytes 1536 | tf_op jit(solution)/shard_map/gather | solution.py:74
  (6 shorter events, 0.0 us)
Async XLA Ops:
  6.5 120.1 %all-gather.4.cloned.1.call-start = ((), (), s32[]{:S(2)}) async-start(), calls=%async_computation.4 | async-start | bytes 4718592 | tf_op jit(solution)/shard_map/all_gather | solution.py:55
  63.5 65.2 %copy-start = (bf16[256,1024]{1,0:T(8,128)(2,1)S(1)}, bf16[256,1024]{1,0:T(8,128)(2,1)}, u32[]{:S(2)}) copy-start(bf16[256,1024]{1,0:T(8,128)(2,1)} %reshape.108) | copy-start | bytes 1572868
  65.5 20.6 %all-to-all-start = ((s32[64,1,4]{2,1,0:T(1,128)}), s32[64,1,4]{2,1,0:T(1,128)S(1)}, u32[]{:S(2)}, u32[]{:S(2)}) async-start(s32[64,1,4]{2,1,0:T(1,128)} %bitcast), calls=%async_computation | async-start | bytes 65536 | tf_op jit(solution)/shard_map/all_to_all | solution.py:43
  86.1 19.1 %all-to-all-start.1 = ((s32[64,1,4]{2,1,0:T(1,128)}), s32[64,1,4]{2,1,0:T(1,128)S(1)}, u32[]{:S(2)}, u32[]{:S(2)}) async-start(s32[64,1,4]{2,1,0:T(1,128)} %bitcast.2), calls=%async_computation.1 | async-start | bytes 65536 | tf_op jit(solution)/shard_map/all_to_all | solution.py:46
  126.6 3.9 %copy-start.1 = (bf16[2048,1024]{1,0:T(8,128)(2,1)S(1)}, bf16[2048,1024]{1,0:T(8,128)(2,1)}, u32[]{:S(2)}) copy-start(bf16[2048,1024]{1,0:T(8,128)(2,1)} %all-gather.4.cloned.1.call-done) | copy-start | bytes 12582916
  132.4 19.4 %all-to-all-start.3 = ((f32[64,1,4]{2,1,0:T(1,128)}), f32[64,1,4]{2,1,0:T(1,128)S(1)}, u32[]{:S(2)}, u32[]{:S(2)}) async-start(f32[64,1,4]{2,1,0:T(1,128)} %bitcast.10), calls=%async_computation.3 | async-start | bytes 65536 | tf_op jit(solution)/shard_map/all_to_all | solution.py:71
Sparse Core Ops, SparseCore 0:
  63.7 30.4 all-gather.3
where the time goes:
time: 162 us
  blocking collectives  70.2 us (43%)
  waiting for transfers between devices  42.3 us (26%)
  starting transfers between devices  15 us (9%)
  between operations  13.5 us (8%)
  local copies, waits for them, and re-layouts  8.9 us (5%)
  other arithmetic  6.85 us (4%)
  matrix products  5.07 us (3%)
    all_to_all x1, blocking collectives, on_device(): lax.all_to_all(send_rows.reshape(groups, capacity, -1), 'dp', split_axis=...  51.2 us
    all_to_all x1, waiting for transfers between devices, on_device(): lax.all_to_all(best_seen.reshape(groups, capacity), 'dp', split_axis=0, c...  14.8 us
    all_to_all x1, waiting for transfers between devices, on_device(): lax.all_to_all(send_order.reshape(groups, capacity), 'dp', split_axis=0,...  14.5 us
    all_to_all x1, waiting for transfers between devices, on_device(): lax.all_to_all(send_labels.reshape(groups, capacity), 'dp', split_axis=0,...  12.9 us
    all_gather x1, blocking collectives, on_device(): lax.all_gather(got_order, 'pair', axis=0, tiled=True)  10.3 us
    all_gather x1, blocking collectives, on_device(): lax.all_gather(got_labels, 'pair', axis=0, tiled=True)  8.77 us
    all_to_all x1, starting transfers between devices, on_device(): lax.all_to_all(send_labels.reshape(groups, capacity), 'dp', split_axis=0,...  5.83 us
    dot_general x4, matrix products, tile_best(): scores = jnp.dot(own_rows, other_rows.T, preferred_element_type=jnp.float32)  5.07 us
  transfers between devices with their start and end apart: 4, of which 3 were waited for; matrix products, arithmetic and copies ran while one was open for 3% of the time, Pallas kernels for 0%

commit v1 on v0

--- a/solution.py
+++ b/solution.py
@@ -53,7 +53,9 @@
     best_seen = jnp.full((slot_count,), -1.0, jnp.float32)
     piece = (
         lax.all_gather(got_rows, "pair", axis=0, tiled=True),
-        lax.all_gather(got_labels, "pair", axis=0, tiled=True),
+        jnp.concatenate(
+            lax.all_to_all(jnp.stack([got_labels] * lax.axis_size("pair")), "pair", 0, 0), axis=0
+        ),
         lax.all_gather(got_order, "pair", axis=0, tiled=True),
     )
     piece_count = piece[0].shape[0]

time: 162 us -> 158 us (0.975)
  the two profiles are of different devices: /device:TPU:8 before, /device:TPU:1 now
where the time goes in v1:
time: 158 us; the launch traced here: 157 us
  blocking collectives  59.8 us (38%)
  waiting for transfers between devices  37.4 us (24%)
  starting transfers between devices  25.4 us (16%)
  between operations  13.5 us (9%)
  local copies, waits for them, and re-layouts  9.4 us (6%)
  other arithmetic  6.84 us (4%)
  matrix products  5.07 us (3%)
    all_to_all x1, blocking collectives, on_device(): lax.all_to_all(send_rows.reshape(groups, capacity, -1), 'dp', split_axis=...  48.9 us
    all_to_all x1, waiting for transfers between devices, on_device(): lax.all_to_all(best_seen.reshape(groups, capacity), 'dp', split_axis=0, c...  13.4 us
    all_to_all x1, waiting for transfers between devices, on_device(): lax.all_to_all(send_order.reshape(groups, capacity), 'dp', split_axis=0,...  12.2 us
    all_to_all x1, waiting for transfers between devices, on_device(): lax.all_to_all(send_labels.reshape(groups, capacity), 'dp', split_axis=0,...  11.8 us
    all_gather x1, blocking collectives, on_device(): lax.all_gather(got_order, 'pair', axis=0, tiled=True)  10.8 us
    all_to_all x1, starting transfers between devices, on_device(): lax.all_to_all(jnp.stack([got_labels] * lax.axis_size('pair')), 'pair', 0...  8.41 us
    all_to_all x1, starting transfers between devices, on_device(): lax.all_to_all(send_labels.reshape(groups, capacity), 'dp', split_axis=0,...  7.86 us
    dot_general x4, matrix products, tile_best(): scores = jnp.dot(own_rows, other_rows.T, preferred_element_type=jnp.float32)  5.07 us
  transfers between devices with their start and end apart: 5, of which 3 were waited for; matrix products, arithmetic and copies ran while one was open for 3% of the time, Pallas kernels for 0%

profile of v1, /device:TPU:1, one launch (start us, length us, event | category | flops | bytes accessed | tf_op | source)
XLA Modules:
  0.0 157.5 jit_solution(15762520729891794870)
XLA Ops:
  6.5 0.0 all-gather.3.cloned.1.call-start
  6.5 0.7 and_select_fusion
  7.2 1.1 fusion.8
  8.3 0.1 fusion.14
  8.4 0.2 reduce_window_sum.11
  8.6 0.2 select_reduce_fusion
  8.7 0.7 compare_select_fusion
  9.4 1.8 %scatter_custom_fusion.2 = bf16[256,1024]{1,0:T(8,128)(2,1)S(1)} fusion(s32[128]{0:T(128)S(1)} %compare_select_fusion, bf16[128,1024]{1,0:T(8,128)(2,1)} %param.3, f32[128]{0:T(128)S(1)} %add_rsqrt_fusion, bf16[]{:T(256)} %constant.18.clone.1), kind=kCustom, calls=%fused_computation.20 | custom fusion | flops 393216 | bytes 786946 | tf_op jit(solution)/shard_map/scatter | solution.py:35
  11.2 0.2 reshape.129
  11.4 48.9 %all_to_all.35 = bf16[64,4,1024]{2,1,0:T(4,128)(2,1)S(1)} all-to-all(bf16[64,4,1024]{2,1,0:T(4,128)(2,1)S(1)} %reshape.129), channel_id=1, replica_groups=mesh['dp'=64,'pair'=8] {'dp'}, dimensions={0} | all-to-all | bytes 1048576 | tf_op jit(solution)/shard_map/all_to_all | solution.py:40
  60.3 0.9 reshape.130
  61.3 0.0 copy-start
  61.3 0.0 all-gather.3.cloned.1.call-update
  61.3 1.2 scatter_custom_fusion
  62.5 0.7 all_to_all.23
  63.2 7.9 %all-to-all-start = ((s32[64,1,4]{2,1,0:T(1,128)}), s32[64,1,4]{2,1,0:T(1,128)S(1)}, u32[]{:S(2)}, u32[]{:S(2)}) async-start(s32[64,1,4]{2,1,0:T(1,128)} %bitcast), calls=%async_computation | async-start | bytes 65536 | tf_op jit(solution)/shard_map/all_to_all | solution.py:43
  71.1 1.1 scatter_custom_fusion.1
  72.2 0.7 all_to_all.26
  72.9 11.8 %all-to-all-done = s32[64,1,4]{2,1,0:T(1,128)S(1)} async-done(((s32[64,1,4]{2,1,0:T(1,128)}), s32[64,1,4]{2,1,0:T(1,128)S(1)}, u32[]{:S(2)}, u32[]{:S(2)}) %all-to-all-start) | async-done | bytes 1056 | tf_op jit(solution)/shard_map/all_to_all | solution.py:43
  84.7 4.5 %all-to-all-start.2 = ((s32[64,1,4]{2,1,0:T(1,128)}), s32[64,1,4]{2,1,0:T(1,128)S(1)}, u32[]{:S(2)}, u32[]{:S(2)}) async-start(s32[64,1,4]{2,1,0:T(1,128)} %bitcast.2), calls=%async_computation.2 | async-start | bytes 65536 | tf_op jit(solution)/shard_map/all_to_all | solution.py:46
  89.2 0.5 broadcast.72
  89.7 0.7 reduce.12
  90.5 0.1 stack.5
  90.6 12.2 %all-to-all-done.2 = s32[64,1,4]{2,1,0:T(1,128)S(1)} async-done(((s32[64,1,4]{2,1,0:T(1,128)}), s32[64,1,4]{2,1,0:T(1,128)S(1)}, u32[]{:S(2)}, u32[]{:S(2)}) %all-to-all-start.2) | async-done | bytes 1056 | tf_op jit(solution)/shard_map/all_to_all | solution.py:46
  102.8 0.6 stack.6
  103.4 8.4 %all-to-all-start.1 = ((s32[8,1,256]{2,1,0:T(1,128)}), s32[8,1,256]{2,1,0:T(1,128)S(1)}, u32[]{:S(2)}, u32[]{:S(2)}) async-start(s32[8,1,256]{2,1,0:T(1,128)} %stack.6), calls=%async_computation.1 | async-start | bytes 16384 | tf_op jit(solution)/shard_map/all_to_all | solution.py:57
  111.8 0.7 reduce.11
  112.5 0.1 reshape.168
  112.6 10.8 %all-gather = s32[8,1,256]{2,1,0:T(1,128)S(1)} all-gather(s32[1,1,256]{2,1,0:T(1,128)S(1)} %reshape.168), channel_id=1, replica_groups=mesh['dp'=64,'pair'=8] {'pair'}, dimensions={0}, use_global_device_ids=true | all-gather | bytes 9216 | tf_op jit(solution)/shard_map/all_gather | solution.py:59
  123.5 0.1 reshape.128
  123.6 0.0 all-to-all-done.1
  123.6 0.0 all-gather.3.cloned.1.call-done
  123.6 0.0 copy-start.1
  123.7 2.1 %fusion.3 = f32[256]{0:T(256)S(1)} fusion(bf16[256,1024]{1,0:T(8,128)(2,1)} %reshape.130, bf16[2048,1024]{1,0:T(8,128)(2,1)} %all-gather.3.cloned.1.call-done, s32[512]{0:T(512)S(1)} %bitcast.23, s32[512]{0:T(512)S(1)} %bitcast.27, pred[256]{0:T(512)(128)(4,1)S(1)} %broadcast_compare_fusion, s32[256]{0:T(256)S(1)} %reshape.128, s32[256]{0:T(256)S(1)} %stack.5), kind=kOutput, calls=%fused_computation.11 | convolution fusion | flops 269221632 | bytes 1580288 | tf_op jit(solution)/shard_map/dot_general | solution.py:10
  125.8 0.0 copy-done
  125.8 1.8 %fusion.2 = f32[256]{0:T(256)S(1)} fusion(bf16[256,1024]{1,0:T(8,128)(2,1)S(1)} %copy-done, bf16[2048,1024]{1,0:T(8,128)(2,1)} %all-gather.3.cloned.1.call-done, s32[512]{0:T(512)S(1)} %bitcast.22, s32[512]{0:T(512)S(1)} %bitcast.26, pred[256]{0:T(512)(128)(4,1)S(1)} %broadcast_compare_fusion, s32[256]{0:T(256)S(1)} %reshape.128, s32[256]{0:T(256)S(1)} %stack.5), kind=kOutput, calls=%fused_computation.10 | convolution fusion | flops 269221632 | bytes 1580288 | tf_op jit(solution)/shard_map/dot_general | solution.py:10
  127.6 0.0 copy-done.1
  127.6 0.6 fusion.1
  128.2 0.6 fusion
  128.7 0.7 max.41
  129.5 4.6 %all-to-all-start.4 = ((f32[64,1,4]{2,1,0:T(1,128)}), f32[64,1,4]{2,1,0:T(1,128)S(1)}, u32[]{:S(2)}, u32[]{:S(2)}) async-start(f32[64,1,4]{2,1,0:T(1,128)} %bitcast.10), calls=%async_computation.4 | async-start | bytes 65536 | tf_op jit(solution)/shard_map/all_to_all | solution.py:73
  134.1 13.4 %all-to-all-done.4 = f32[64,1,4]{2,1,0:T(1,128)S(1)} async-done(((f32[64,1,4]{2,1,0:T(1,128)}), f32[64,1,4]{2,1,0:T(1,128)S(1)}, u32[]{:S(2)}, u32[]{:S(2)}) %all-to-all-start.4) | async-done | bytes 1056 | tf_op jit(solution)/shard_map/all_to_all | solution.py:73
  147.5 0.5 broadcast.74
  148.0 0.7 reduce.13
  148.7 0.1 reshape.131
  148.8 1.8 %gather_fusion = f32[128]{0:T(128)} fusion(f32[256]{0:T(256)S(1)} %reshape.131, s32[1024]{0:T(1024)S(1)} %pad_clamp_fusion), kind=kCustom, calls=%fused_computation | custom fusion | bytes 1536 | tf_op jit(solution)/shard_map/gather | solution.py:76
  (6 shorter events, 0.0 us)
Async XLA Ops:
  6.5 117.1 %all-gather.3.cloned.1.call-start = ((), (), s32[]{:S(2)}) async-start(), calls=%async_computation.5 | async-start | bytes 4718592 | tf_op jit(solution)/shard_map/all_gather | solution.py:55
  61.3 64.5 %copy-start = (bf16[256,1024]{1,0:T(8,128)(2,1)S(1)}, bf16[256,1024]{1,0:T(8,128)(2,1)}, u32[]{:S(2)}) copy-start(bf16[256,1024]{1,0:T(8,128)(2,1)} %reshape.130) | copy-start | bytes 1572868
  63.2 21.5 %all-to-all-start = ((s32[64,1,4]{2,1,0:T(1,128)}), s32[64,1,4]{2,1,0:T(1,128)S(1)}, u32[]{:S(2)}, u32[]{:S(2)}) async-start(s32[64,1,4]{2,1,0:T(1,128)} %bitcast), calls=%async_computation | async-start | bytes 65536 | tf_op jit(solution)/shard_map/all_to_all | solution.py:43
  84.7 18.1 %all-to-all-start.2 = ((s32[64,1,4]{2,1,0:T(1,128)}), s32[64,1,4]{2,1,0:T(1,128)S(1)}, u32[]{:S(2)}, u32[]{:S(2)}) async-start(s32[64,1,4]{2,1,0:T(1,128)} %bitcast.2), calls=%async_computation.2 | async-start | bytes 65536 | tf_op jit(solution)/shard_map/all_to_all | solution.py:46
  103.4 20.2 %all-to-all-start.1 = ((s32[8,1,256]{2,1,0:T(1,128)}), s32[8,1,256]{2,1,0:T(1,128)S(1)}, u32[]{:S(2)}, u32[]{:S(2)}) async-start(s32[8,1,256]{2,1,0:T(1,128)} %stack.6), calls=%async_computation.1 | async-start | bytes 16384 | tf_op jit(solution)/shard_map/all_to_all | solution.py:57
  123.6 3.9 %copy-start.1 = (bf16[2048,1024]{1,0:T(8,128)(2,1)S(1)}, bf16[2048,1024]{1,0:T(8,128)(2,1)}, u32[]{:S(2)}) copy-start(bf16[2048,1024]{1,0:T(8,128)(2,1)} %all-gather.3.cloned.1.call-done) | copy-start | bytes 12582916
  129.5 18.0 %all-to-all-start.4 = ((f32[64,1,4]{2,1,0:T(1,128)}), f32[64,1,4]{2,1,0:T(1,128)S(1)}, u32[]{:S(2)}, u32[]{:S(2)}) async-start(f32[64,1,4]{2,1,0:T(1,128)} %bitcast.10), calls=%async_computation.4 | async-start | bytes 65536 | tf_op jit(solution)/shard_map/all_to_all | solution.py:73
Sparse Core Ops, SparseCore 0:
  61.4 35.0 all-gather.2
